TPU v7x, 256 devices: a whole 4x4x8 slice. The times are simulated.
256 devices in a mesh: gx: 32 (over x, z), gy: 8 (over y, core).
Axes of the slice: x: 4, y: 4, z: 8, core: 2. Of those that a mesh axis runs over, the one named last changes fastest.
Arguments:
- field: bfloat16 [3, 1, 48, 256, 1024], P(None, None, None, 'gx', 'gy'), may hold values from -6 to 6
- weight_x: bfloat16 [15, 48, 48], replicated, may hold values from -0.21875 to 0.21875
- weight_y: bfloat16 [15, 48, 48], replicated, may hold values from -0.21875 to 0.21875
- cotangent: bfloat16 [3, 1, 48, 256, 1024], P(None, None, None, 'gx', 'gy'), may hold values from -6 to 6
Outputs:
- output: bfloat16 [3, 1, 48, 256, 1024], P(None, None, None, 'gx', 'gy')
- field_grad: bfloat16 [3, 1, 48, 256, 1024], P(None, None, None, 'gx', 'gy')
- wx_grad: float32 [15, 48, 48], replicated
- wy_grad: float32 [15, 48, 48], replicated
All inputs are finite; a program needn't handle non-finite values.
Results may differ from a plain program's by a relative error of at most 0.0054.
Values may be sent and summed in bfloat16 or wider, within the bound.
No kernel may reach another device: no remote copies, remote signals or barrier semaphores. Data moves between devices by JAX's collectives and lax.ppermute only.
A program may use at most 64 MiB of HBM per device.

v0:
```python
import jax
import jax.numpy as jnp
from jax import lax
from jax.sharding import PartitionSpec as P


def with_halo(cells, sides, width):
    for axis, dim in sides:
        count = lax.axis_size(axis)
        ends = count - 1
        head = lax.slice_in_dim(cells, 0, width, axis=dim)
        tail = lax.slice_in_dim(cells, cells.shape[dim] - width, cells.shape[dim], axis=dim)
        cells = jnp.concatenate(
            [
                lax.ppermute(tail, axis, [(i, (i + 1) % count) for i in range(ends)]),
                cells,
                lax.ppermute(head, axis, [((i + 1) % count, i) for i in range(ends)]),
            ],
            axis=dim,
        )
    return cells


def conv_padded(padded, weight, dim):
    taps = weight.shape[0]
    length = padded.shape[dim] - taps + 1
    total = None
    for tap in range(taps):
        piece = lax.slice_in_dim(padded, tap, tap + length, axis=dim)
        term = jnp.einsum("bzcxy,co->bzoxy", piece, weight[tap], preferred_element_type=jnp.float32)
        total = term if total is None else total + term
    return total


def flipped(weight):
    return jnp.transpose(jnp.flip(weight, 0), (0, 2, 1))


def tap_products(padded, grads, taps, dim):
    length = grads.shape[dim]
    terms = []
    for tap in range(taps):
        piece = lax.slice_in_dim(padded, tap, tap + length, axis=dim)
        terms.append(
            jnp.einsum("bzcxy,bzoxy->co", piece, grads, preferred_element_type=jnp.float32)
        )
    return jnp.stack(terms)


def activate(pre):
    return jax.nn.gelu(pre.astype(jnp.float32)).astype(jnp.bfloat16)


def y_reach(values, half):
    return with_halo(values, (("gy", 4),), half)


def per_device(field, weight_x, weight_y, cotangent):
    taps = weight_x.shape[0]
    half = (taps - 1) // 2
    lines = lax.all_to_all(field, "gx", split_axis=4, concat_axis=3, tiled=True)
    lines_pad = jnp.pad(lines, ((0, 0), (0, 0), (0, 0), (half, half), (0, 0)))
    pre_lines = lax.optimization_barrier(conv_padded(lines_pad, weight_x, 3).astype(jnp.bfloat16))
    act_lines = activate(pre_lines)
    act, pre = (
        lax.all_to_all(act_lines, "gx", split_axis=3, concat_axis=4, tiled=True),
        lax.all_to_all(pre_lines, "gx", split_axis=3, concat_axis=4, tiled=True),
    )
    act_pad = y_reach(act, half)
    output = (field.astype(jnp.float32) + conv_padded(act_pad, weight_y, 4)).astype(jnp.bfloat16)
    grad_pad = y_reach(cotangent, half)
    act_grad = conv_padded(grad_pad, flipped(weight_y), 4)
    _, pull = jax.vjp(jax.nn.gelu, pre.astype(jnp.float32))
    pre_grad = pull(act_grad)[0].astype(jnp.bfloat16)
    wy_term = tap_products(act_pad, cotangent, taps, 4)
    paired = with_halo(jnp.stack((field, pre_grad)), (("gx", 4),), half)
    field_pad = paired[0]
    grad_xpad = paired[1]
    field_grad = (
        cotangent.astype(jnp.float32) + conv_padded(grad_xpad, flipped(weight_x), 3)
    ).astype(jnp.bfloat16)
    wx_term = tap_products(field_pad, pre_grad, taps, 3)
    wx_sum, wy_sum = lax.psum((wx_term, wy_term), ("gx", "gy"))
    count = (
        field.shape[0]
        * field.shape[1]
        * field.shape[3]
        * field.shape[4]
        * lax.axis_size("gx")
        * lax.axis_size("gy")
    )
    factor = 1.0 / jnp.sqrt(jnp.float32(count))
    return (output, field_grad, wx_sum * factor, wy_sum * factor)


def solution(mesh):
    in_specs = (P(None, None, None, "gx", "gy"), P(), P(), P(None, None, None, "gx", "gy"))
    out_specs = (P(None, None, None, "gx", "gy"), P(None, None, None, "gx", "gy"), P(), P())
    return jax.shard_map(
        per_device, mesh=mesh, in_specs=in_specs, out_specs=out_specs, check_vma=False
    )
```

profile of v0, /device:TPU:8, one launch (start us, length us, event | category | flops | bytes accessed | tf_op | source)
XLA Modules:
  0.0 378.1 jit_solution(10416243189057325038)
XLA Ops:
  7.2 1.6 copy.144
  8.8 1.7 reshape.644
  10.5 11.3 %all-to-all-start = ((bf16[32,2,2304]{2,1,0:T(2,128)(2,1)}), bf16[32,2,2304]{2,1,0:T(2,128)(2,1)S(1)}, u32[]{:S(2)}, u32[]{:S(2)}) async-start(bf16[32,2,2304]{2,1,0:T(2,128)(2,1)} %reshape.644), calls=%async_computation | async-start | bytes 589824 | tf_op jit(solution)/shard_map/all_to_all | solution.py:61
  22.1 1.9 collective-permute-start.3
  24.0 2.4 collective-permute-start.2
  26.7 0.7 reverse_bitcast_fusion
  27.4 0.8 copy.389
  28.1 3.9 %collective-permute-done.2 = bf16[3,1,48,8,7]{4,2,3,0,1:T(8,128)(2,1)S(1)} collective-permute-done((bf16[3,1,48,8,7]{4,2,3,0,1:T(8,128)(2,1)S(1)}, bf16[3,1,48,8,7]{4,2,3,0,1:T(8,128)(2,1)S(1)}, u32[]{:S(2)}, u32[]{:S(2)}) %collective-permute-start.2) | collective-permute-done | bytes 16160 | tf_op jit(solution)/shard_map/ppermute | solution.py:15
  32.1 0.4 fusion.110
  32.8 0.4 convolution_add_fusion.18
  33.1 0.4 convolution_add_fusion.17
  33.5 0.4 convolution_add_fusion.16
  33.9 0.4 convolution_add_fusion.15
  34.3 0.4 fusion.19
  35.1 1.1 fusion.6
  36.2 0.8 reshape.645
  39.8 0.4 convolution_add_fusion.39
  42.6 0.6 copy.165
  43.2 1.7 reshape.646
  44.9 10.0 %all-to-all-start.1 = ((bf16[32,2,2304]{2,1,0:T(2,128)(2,1)}), bf16[32,2,2304]{2,1,0:T(2,128)(2,1)S(1)}, u32[]{:S(2)}, u32[]{:S(2)}) async-start(bf16[32,2,2304]{2,1,0:T(2,128)(2,1)} %reshape.646), calls=%async_computation.1 | async-start | bytes 589824 | tf_op jit(solution)/shard_map/all_to_all | solution.py:66
  54.9 1.0 fusion.5
  55.9 1.0 fusion.4
  56.9 1.0 fusion.3
  57.9 0.6 copy.196
  58.5 1.7 reshape.648
  60.2 6.9 %all-to-all-done.1 = bf16[32,2,2304]{2,1,0:T(2,128)(2,1)S(1)} async-done(((bf16[32,2,2304]{2,1,0:T(2,128)(2,1)}), bf16[32,2,2304]{2,1,0:T(2,128)(2,1)S(1)}, u32[]{:S(2)}, u32[]{:S(2)}) %all-to-all-start.1) | async-done | bytes 294944 | tf_op jit(solution)/shard_map/all_to_all | solution.py:66
  67.1 4.7 %all-to-all-start.2 = ((bf16[32,2,2304]{2,1,0:T(2,128)(2,1)}), bf16[32,2,2304]{2,1,0:T(2,128)(2,1)S(1)}, u32[]{:S(2)}, u32[]{:S(2)}) async-start(bf16[32,2,2304]{2,1,0:T(2,128)(2,1)} %reshape.648), calls=%async_computation.2 | async-start | bytes 589824 | tf_op jit(solution)/shard_map/all_to_all | solution.py:67
  71.9 1.9 fusion.2
  73.7 0.8 reshape.647
  74.8 0.5 copy.168
  75.3 0.5 copy.179
  75.8 0.9 fusion.299
  76.7 1.9 collective-permute-start.1
  78.6 2.4 collective-permute-start
  81.0 1.1 fusion.178
  82.1 1.3 all-to-all-done.2
  83.4 0.8 reshape.649
  84.6 1.3 copy.202
  85.9 1.9 fusion.65
  87.9 3.8 %collective-permute-start.4 = (bf16[2,3,1,48,7,128]{5,3,4,1,2,0:T(8,128)(2,1)S(1)}, bf16[2,3,1,48,7,128]{5,3,4,1,2,0:T(8,128)(2,1)S(1)}, u32[]{:S(2)}, u32[]{:S(2)}) collective-permute-start(bf16[2,3,1,48,7,128]{5,3,4,1,2,0:T(8,128)(2,1)S(1)} %get-tuple-element.20), channel_id=1, source_target_pairs={{0,8},{8,16},{16,24},{24,32},{32,40},{40,48},{48,56},{56,64},{64,7... | collective-permute-start | bytes 1548296 | tf_op jit(solution)/shard_map/ppermute | solution.py:15
  91.7 1.5 collective-permute-start.5
  93.9 0.4 fusion.39
  94.3 0.4 fusion.38
  95.0 0.4 fusion.36
  95.4 0.4 fusion.35
  96.0 0.4 fusion.185
  98.1 0.4 convolution_add_fusion.31
  98.5 0.4 convolution_add_fusion.30
  98.9 0.4 convolution_add_fusion.29
  99.3 0.4 convolution_add_fusion.28
  100.0 0.4 fusion
  100.4 0.4 convolution_add_fusion.26
  100.8 0.4 convolution_add_fusion.25
  101.2 0.4 convolution_add_fusion.24
  101.6 0.4 convolution_add_fusion.23
  102.0 0.4 convolution_add_fusion.22
  102.4 0.4 convolution_add_fusion.21
  102.9 0.4 fusion.23
  103.7 0.8 copy.220
  105.2 0.7 copy-done.13
  105.9 0.6 collective-permute-done.5
  113.8 0.8 copy.221
  114.6 254.6 %all-reduce.4.cloned.1.call-done = (f32[15,48,48]{2,1,0:T(8,128)}, f32[15,48,48]{2,1,0:T(8,128)}) async-done(((f32[15,48,48]{2,1,0:T(8,128)}, f32[15,48,48]{2,1,0:T(8,128)}), (f32[15,48,48]{2,1,0:T(8,128)}, f32[15,48,48]{2,1,0:T(8,128)})) %all-reduce.4.cloned.1.call-update) | async-done | bytes 276496 | tf_op jit(solution)/shard_map/psum | solution.py:83
  369.2 2.0 broadcast_multiply_fusion
  (110 shorter events, 18.5 us)
Async XLA Ops:
  7.2 14.7 %copy-start = (bf16[3,1,48,8,128]{4,3,2,1,0:T(8,128)(2,1)S(1)}, bf16[3,1,48,8,128]{4,3,2,1,0:T(8,128)(2,1)}, u32[]{:S(2)}) copy-start(bf16[3,1,48,8,128]{4,3,2,1,0:T(8,128)(2,1)} %param.7) | copy-start | bytes 884740
  8.8 17.7 %copy-start.9 = (bf16[15,48,48]{2,1,0:T(8,128)(2,1)S(1)}, bf16[15,48,48]{2,1,0:T(8,128)(2,1)}, u32[]{:S(2)}) copy-start(bf16[15,48,48]{2,1,0:T(8,128)(2,1)} %param.6) | copy-start | bytes 207364
  10.5 25.7 %all-to-all-start = ((bf16[32,2,2304]{2,1,0:T(2,128)(2,1)}), bf16[32,2,2304]{2,1,0:T(2,128)(2,1)S(1)}, u32[]{:S(2)}, u32[]{:S(2)}) async-start(bf16[32,2,2304]{2,1,0:T(2,128)(2,1)} %reshape.644), calls=%async_computation | async-start | bytes 589824 | tf_op jit(solution)/shard_map/all_to_all | solution.py:61
  21.8 4.9 %copy-start.8 = (bf16[15,48,48]{2,1,0:T(8,128)(2,1)S(1)}, bf16[15,48,48]{2,1,0:T(8,128)(2,1)}, u32[]{:S(2)}) copy-start(bf16[15,48,48]{2,1,0:T(8,128)(2,1)} %param.5) | copy-start | bytes 207364
  21.9 5.5 %copy-start.2 = (bf16[3,1,48,8,128]{4,3,2,1,0:T(8,128)(2,1)S(1)}, bf16[3,1,48,8,128]{4,3,2,1,0:T(8,128)(2,1)}, u32[]{:S(2)}) copy-start(bf16[3,1,48,8,128]{4,3,2,1,0:T(8,128)(2,1)} %param.4) | copy-start | bytes 884740
  22.1 12.6 %collective-permute-start.3 = (bf16[3,1,48,8,7]{4,2,3,0,1:T(8,128)(2,1)S(1)}, bf16[3,1,48,8,7]{4,2,3,0,1:T(8,128)(2,1)S(1)}, u32[]{:S(2)}, u32[]{:S(2)}) collective-permute-start(bf16[3,1,48,8,7]{4,2,3,0,1:T(8,128)(2,1)S(1)} %get-tuple-element.22), channel_id=1, source_target_pairs={{1,0},{2,1},{3,2},{4,3},{5,4},{6,5},{7,6},{9,8},{10,9},{11,10},{12... | collective-permute-start | bytes 48392 | tf_op jit(solution)/shard_map/ppermute | solution.py:17
  24.0 8.0 %collective-permute-start.2 = (bf16[3,1,48,8,7]{4,2,3,0,1:T(8,128)(2,1)S(1)}, bf16[3,1,48,8,7]{4,2,3,0,1:T(8,128)(2,1)S(1)}, u32[]{:S(2)}, u32[]{:S(2)}) collective-permute-start(bf16[3,1,48,8,7]{4,2,3,0,1:T(8,128)(2,1)S(1)} %get-tuple-element.23), channel_id=1, source_target_pairs={{0,1},{1,2},{2,3},{3,4},{4,5},{5,6},{6,7},{8,9},{9,10},{10,11},{11... | collective-permute-start | bytes 48392 | tf_op jit(solution)/shard_map/ppermute | solution.py:15
  26.5 8.6 %copy-start.12 = (bf16[15,48,48]{1,2,0:T(8,128)(2,1)}, bf16[15,48,48]{1,2,0:T(8,128)(2,1)S(1)}, u32[]{:S(2)}) copy-start(bf16[15,48,48]{1,2,0:T(8,128)(2,1)S(1)} %reverse_bitcast_fusion.1) | copy-start | bytes 207364
  42.4 12.5 %copy-start.5 = (f32[48,3,8,128]{3,0,2,1:T(8,128)S(1)}, f32[48,3,8,128]{3,0,2,1:T(8,128)}, u32[]{:S(2)}) copy-start(f32[48,3,8,128]{3,0,2,1:T(8,128)} %fusion.6) | copy-start | bytes 1769476
  44.9 22.2 %all-to-all-start.1 = ((bf16[32,2,2304]{2,1,0:T(2,128)(2,1)}), bf16[32,2,2304]{2,1,0:T(2,128)(2,1)S(1)}, u32[]{:S(2)}, u32[]{:S(2)}) async-start(bf16[32,2,2304]{2,1,0:T(2,128)(2,1)} %reshape.646), calls=%async_computation.1 | async-start | bytes 589824 | tf_op jit(solution)/shard_map/all_to_all | solution.py:66
  67.1 16.3 %all-to-all-start.2 = ((bf16[32,2,2304]{2,1,0:T(2,128)(2,1)}), bf16[32,2,2304]{2,1,0:T(2,128)(2,1)S(1)}, u32[]{:S(2)}, u32[]{:S(2)}) async-start(bf16[32,2,2304]{2,1,0:T(2,128)(2,1)} %reshape.648), calls=%async_computation.2 | async-start | bytes 589824 | tf_op jit(solution)/shard_map/all_to_all | solution.py:67
  71.8 297.4 %all-reduce.4.cloned.1.call-start = ((), (), s32[]{:S(2)}) async-start(), calls=%async_computation.3 | async-start | bytes 1474560 | tf_op jit(solution)/shard_map/psum | solution.py:83
  74.8 6.2 %copy-start.10 = (bf16[15,48,48]{2,1,0:T(8,128)(2,1)S(1)}, bf16[15,48,48]{2,1,0:T(8,128)(2,1)}, u32[]{:S(2)}) copy-start(bf16[15,48,48]{2,1,0:T(8,128)(2,1)} %param.6) | copy-start | bytes 207364
  75.8 8.4 %copy-start.6 = (bf16[3,48,8,128]{3,1,2,0:T(8,128)(2,1)}, bf16[3,48,8,128]{3,1,2,0:T(8,128)(2,1)S(1)}, u32[]{:S(2)}) copy-start(bf16[3,48,8,128]{3,1,2,0:T(8,128)(2,1)S(1)} %copy.179) | copy-start | bytes 884740
  76.7 19.7 %collective-permute-start.1 = (bf16[3,1,48,8,7]{4,2,3,0,1:T(8,128)(2,1)}, bf16[3,1,48,8,7]{4,2,3,0,1:T(8,128)(2,1)S(1)}, u32[]{:S(2)}, u32[]{:S(2)}) collective-permute-start(bf16[3,1,48,8,7]{4,2,3,0,1:T(8,128)(2,1)} %get-tuple-element.26), channel_id=1, source_target_pairs={{1,0},{2,1},{3,2},{4,3},{5,4},{6,5},{7,6},{9,8},{10,9},{11,10},{12... | collective-permute-start | bytes 48392 | tf_op jit(solution)/shard_map/ppermute | solution.py:17
  78.6 14.6 %collective-permute-start = (bf16[3,1,48,8,7]{4,2,3,0,1:T(8,128)(2,1)}, bf16[3,1,48,8,7]{4,2,3,0,1:T(8,128)(2,1)S(1)}, u32[]{:S(2)}, u32[]{:S(2)}) collective-permute-start(bf16[3,1,48,8,7]{4,2,3,0,1:T(8,128)(2,1)} %get-tuple-element.27), channel_id=1, source_target_pairs={{0,1},{1,2},{2,3},{3,4},{4,5},{5,6},{6,7},{8,9},{9,10},{10,11},{11... | collective-permute-start | bytes 48392 | tf_op jit(solution)/shard_map/ppermute | solution.py:15
  85.9 1.9 copy-start.1
  87.9 17.3 %collective-permute-start.4 = (bf16[2,3,1,48,7,128]{5,3,4,1,2,0:T(8,128)(2,1)S(1)}, bf16[2,3,1,48,7,128]{5,3,4,1,2,0:T(8,128)(2,1)S(1)}, u32[]{:S(2)}, u32[]{:S(2)}) collective-permute-start(bf16[2,3,1,48,7,128]{5,3,4,1,2,0:T(8,128)(2,1)S(1)} %get-tuple-element.20), channel_id=1, source_target_pairs={{0,8},{8,16},{16,24},{24,32},{32,40},{40,48},{48,56},{56,64},{64,7... | collective-permute-start | bytes 1548296 | tf_op jit(solution)/shard_map/ppermute | solution.py:15
  91.7 14.8 %collective-permute-start.5 = (bf16[2,3,1,48,7,128]{5,3,4,1,2,0:T(8,128)(2,1)S(1)}, bf16[2,3,1,48,7,128]{5,3,4,1,2,0:T(8,128)(2,1)S(1)}, u32[]{:S(2)}, u32[]{:S(2)}) collective-permute-start(bf16[2,3,1,48,7,128]{5,3,4,1,2,0:T(8,128)(2,1)S(1)} %get-tuple-element.21), channel_id=1, source_target_pairs={{8,0},{16,8},{24,16},{32,24},{40,32},{48,40},{56,48},{64,56},{72,6... | collective-permute-start | bytes 1548296 | tf_op jit(solution)/shard_map/ppermute | solution.py:17
  94.6 1.1 copy-start.7
  98.9 1.1 copy-start.4
  102.0 1.0 copy-start.3
  105.2 0.7 copy-start.13
  109.3 1.2 copy-start.11
  110.4 0.7 copy-start.14
Sparse Core Ops, SparseCore 0:
  113.7 255.4 all-reduce.3
where the time goes:
time: 379 us; the launch traced here: 378 us
  waiting for transfers between devices  267 us (70%)
  starting transfers between devices  40 us (11%)
  matrix products  33.7 us (9%)
  local copies, waits for them, and re-layouts  19.4 us (5%)
  between operations  15.2 us (4%)
    psum x1, waiting for transfers between devices, per_device(): wx_sum, wy_sum = lax.psum((wx_term, wy_term), ('gx', 'gy'))  255 us
    dot_general x60, matrix products, conv_padded(): jnp.einsum('bzcxy,co->bzoxy', piece, weight[tap], preferred_element_type=...  25.2 us
    unnamed x41, local copies, waits for them, and re-layouts  12.9 us
    all_to_all x1, starting transfers between devices, per_device(): lines = lax.all_to_all(field, 'gx', split_axis=4, concat_axis=3, tiled=True)  11.3 us
    all_to_all x1, starting transfers between devices, per_device(): lax.all_to_all(act_lines, 'gx', split_axis=3, concat_axis=4, tiled=True)  9.97 us
    ppermute x3, starting transfers between devices, with_halo(): lax.ppermute(tail, axis, [(i, (i + 1) % count) for i in range(ends)])  8.62 us
    dot_general x30, matrix products, tap_products(): jnp.einsum('bzcxy,bzoxy->co', piece, grads, preferred_element_type=jnp.fl...  8.47 us
  transfers between devices with their start and end apart: 10, of which 5 were waited for; matrix products, arithmetic and copies ran while one was open for 9% of the time, Pallas kernels for 0%

commit v1 on v0

--- a/solution.py
+++ b/solution.py
@@ -2,6 +2,11 @@
 import jax.numpy as jnp
 from jax import lax
 from jax.sharding import PartitionSpec as P
+
+
+def by_each_axis(array, first, second):
+    partial = lax.psum(array, first)
+    return lax.psum(partial, second)
 
 
 def with_halo(cells, sides, width):
@@ -80,7 +85,7 @@
         cotangent.astype(jnp.float32) + conv_padded(grad_xpad, flipped(weight_x), 3)
     ).astype(jnp.bfloat16)
     wx_term = tap_products(field_pad, pre_grad, taps, 3)
-    wx_sum, wy_sum = lax.psum((wx_term, wy_term), ("gx", "gy"))
+    wx_sum, wy_sum = by_each_axis((wx_term, wy_term), "gy", "gx")
     count = (
         field.shape[0]
         * field.shape[1]

time: 379 us -> 342 us (0.902)
  waiting for transfers between devices: 267 us -> 231 us
    psum x1 -> x2, waiting for transfers between devices: 255 us -> 218 us  [the longest x1 152 us: by_each_axis(): return lax.psum(partial, second)]
  transfers between devices with their start and end apart: 10 -> 11, of which waited for: 5 -> 6; matrix products, arithmetic and copies ran while one was open for 9% -> 10% of each run, Pallas kernels for 0% -> 0%
where the time goes in v1:
time: 342 us
  waiting for transfers between devices  231 us (68%)
  starting transfers between devices  40 us (12%)
  matrix products  33.7 us (10%)
  local copies, waits for them, and re-layouts  19.4 us (6%)
  between operations  15.2 us (4%)
    psum x1, waiting for transfers between devices, by_each_axis(): return lax.psum(partial, second)  152 us
    psum x1, waiting for transfers between devices, by_each_axis(): partial = lax.psum(array, first)  65.6 us
    dot_general x60, matrix products, conv_padded(): jnp.einsum('bzcxy,co->bzoxy', piece, weight[tap], preferred_element_type=...  25.2 us
    unnamed x41, local copies, waits for them, and re-layouts  12.9 us
    all_to_all x1, starting transfers between devices, per_device(): lines = lax.all_to_all(field, 'gx', split_axis=4, concat_axis=3, tiled=True)  11.3 us
    all_to_all x1, starting transfers between devices, per_device(): lax.all_to_all(act_lines, 'gx', split_axis=3, concat_axis=4, tiled=True)  9.96 us
    ppermute x3, starting transfers between devices, with_halo(): lax.ppermute(tail, axis, [(i, (i + 1) % count) for i in range(ends)])  8.62 us
    dot_general x30, matrix products, tap_products(): jnp.einsum('bzcxy,bzoxy->co', piece, grads, preferred_element_type=jnp.fl...  8.47 us
  transfers between devices with their start and end apart: 11, of which 6 were waited for; matrix products, arithmetic and copies ran while one was open for 10% of the time, Pallas kernels for 0%

profile of v1, /device:TPU:8, one launch (start us, length us, event | category | flops | bytes accessed | tf_op | source)
XLA Modules:
  0.0 341.6 jit_solution(9048228014717731848)
XLA Ops:
  7.2 1.6 copy.144
  8.8 1.7 reshape.644
  10.5 11.3 %all-to-all-start = ((bf16[32,2,2304]{2,1,0:T(2,128)(2,1)}), bf16[32,2,2304]{2,1,0:T(2,128)(2,1)S(1)}, u32[]{:S(2)}, u32[]{:S(2)}) async-start(bf16[32,2,2304]{2,1,0:T(2,128)(2,1)} %reshape.644), calls=%async_computation | async-start | bytes 589824 | tf_op jit(solution)/shard_map/all_to_all | solution.py:66
  22.1 1.9 collective-permute-start.3
  24.0 2.4 collective-permute-start.2
  26.7 0.7 reverse_bitcast_fusion
  27.4 0.8 copy.389
  28.2 3.9 %collective-permute-done.2 = bf16[3,1,48,8,7]{4,2,3,0,1:T(8,128)(2,1)S(1)} collective-permute-done((bf16[3,1,48,8,7]{4,2,3,0,1:T(8,128)(2,1)S(1)}, bf16[3,1,48,8,7]{4,2,3,0,1:T(8,128)(2,1)S(1)}, u32[]{:S(2)}, u32[]{:S(2)}) %collective-permute-start.2) | collective-permute-done | bytes 16160 | tf_op jit(solution)/shard_map/ppermute | solution.py:20
  32.1 0.4 fusion.110
  32.8 0.4 convolution_add_fusion.18
  33.1 0.4 convolution_add_fusion.17
  33.5 0.4 convolution_add_fusion.16
  33.9 0.4 convolution_add_fusion.15
  34.3 0.4 fusion.19
  35.1 1.1 fusion.6
  36.2 0.8 reshape.645
  39.8 0.4 convolution_add_fusion.39
  42.6 0.6 copy.165
  43.2 1.7 reshape.646
  44.9 10.0 %all-to-all-start.1 = ((bf16[32,2,2304]{2,1,0:T(2,128)(2,1)}), bf16[32,2,2304]{2,1,0:T(2,128)(2,1)S(1)}, u32[]{:S(2)}, u32[]{:S(2)}) async-start(bf16[32,2,2304]{2,1,0:T(2,128)(2,1)} %reshape.646), calls=%async_computation.1 | async-start | bytes 589824 | tf_op jit(solution)/shard_map/all_to_all | solution.py:71
  54.9 1.0 fusion.5
  55.9 1.0 fusion.4
  56.9 1.0 fusion.3
  57.9 0.6 copy.196
  58.5 1.7 reshape.648
  60.2 6.9 %all-to-all-done.1 = bf16[32,2,2304]{2,1,0:T(2,128)(2,1)S(1)} async-done(((bf16[32,2,2304]{2,1,0:T(2,128)(2,1)}), bf16[32,2,2304]{2,1,0:T(2,128)(2,1)S(1)}, u32[]{:S(2)}, u32[]{:S(2)}) %all-to-all-start.1) | async-done | bytes 294944 | tf_op jit(solution)/shard_map/all_to_all | solution.py:71
  67.1 4.7 %all-to-all-start.2 = ((bf16[32,2,2304]{2,1,0:T(2,128)(2,1)}), bf16[32,2,2304]{2,1,0:T(2,128)(2,1)S(1)}, u32[]{:S(2)}, u32[]{:S(2)}) async-start(bf16[32,2,2304]{2,1,0:T(2,128)(2,1)} %reshape.648), calls=%async_computation.2 | async-start | bytes 589824 | tf_op jit(solution)/shard_map/all_to_all | solution.py:72
  71.9 1.9 fusion.2
  73.7 0.8 reshape.647
  74.8 0.5 copy.168
  75.3 0.5 copy.179
  75.8 0.9 fusion.299
  76.7 1.9 collective-permute-start.1
  78.6 2.4 collective-permute-start
  81.0 1.1 fusion.178
  82.1 1.3 all-to-all-done.2
  83.4 0.8 reshape.649
  84.6 1.3 copy.202
  85.9 1.9 fusion.65
  87.9 3.8 %collective-permute-start.4 = (bf16[2,3,1,48,7,128]{5,3,4,1,2,0:T(8,128)(2,1)S(1)}, bf16[2,3,1,48,7,128]{5,3,4,1,2,0:T(8,128)(2,1)S(1)}, u32[]{:S(2)}, u32[]{:S(2)}) collective-permute-start(bf16[2,3,1,48,7,128]{5,3,4,1,2,0:T(8,128)(2,1)S(1)} %get-tuple-element.22), channel_id=1, source_target_pairs={{0,8},{8,16},{16,24},{24,32},{32,40},{40,48},{48,56},{56,64},{64,7... | collective-permute-start | bytes 1548296 | tf_op jit(solution)/shard_map/ppermute | solution.py:20
  91.7 1.5 collective-permute-start.5
  93.9 0.4 fusion.39
  94.3 0.4 fusion.38
  95.4 0.4 fusion.35
  96.0 0.4 fusion.185
  98.2 0.4 convolution_add_fusion.31
  98.5 0.4 convolution_add_fusion.30
  98.9 0.4 convolution_add_fusion.29
  99.3 0.4 convolution_add_fusion.28
  100.0 0.4 fusion
  100.4 0.4 convolution_add_fusion.26
  100.8 0.4 convolution_add_fusion.25
  101.2 0.4 convolution_add_fusion.24
  101.6 0.4 convolution_add_fusion.23
  102.0 0.4 convolution_add_fusion.22
  102.4 0.4 convolution_add_fusion.21
  102.9 0.4 fusion.23
  103.7 0.8 copy.220
  105.2 0.7 copy-done.13
  106.0 0.6 collective-permute-done.5
  113.5 65.6 %all-reduce.8.cloned.1.call-done = (f32[15,48,48]{2,1,0:T(8,128)}, f32[15,48,48]{2,1,0:T(8,128)}) async-done(((f32[15,48,48]{2,1,0:T(8,128)}, f32[15,48,48]{2,1,0:T(8,128)}), (f32[15,48,48]{2,1,0:T(8,128)}, f32[15,48,48]{2,1,0:T(8,128)})) %all-reduce.8.cloned.1.call-update) | async-done | bytes 276496 | tf_op jit(solution)/shard_map/psum | solution.py:8
  179.6 0.8 copy.221
  180.4 152.3 %all-reduce.6.cloned.1.call-done = (f32[15,48,48]{2,1,0:T(8,128)}, f32[15,48,48]{2,1,0:T(8,128)}) async-done(((f32[15,48,48]{2,1,0:T(8,128)}, f32[15,48,48]{2,1,0:T(8,128)}), (f32[15,48,48]{2,1,0:T(8,128)}, f32[15,48,48]{2,1,0:T(8,128)})) %all-reduce.6.cloned.1.call-update) | async-done | bytes 276496 | tf_op jit(solution)/shard_map/psum | solution.py:9
  332.7 2.0 broadcast_multiply_fusion
  (113 shorter events, 18.9 us)
Async XLA Ops:
  7.2 14.7 %copy-start = (bf16[3,1,48,8,128]{4,3,2,1,0:T(8,128)(2,1)S(1)}, bf16[3,1,48,8,128]{4,3,2,1,0:T(8,128)(2,1)}, u32[]{:S(2)}) copy-start(bf16[3,1,48,8,128]{4,3,2,1,0:T(8,128)(2,1)} %param.7) | copy-start | bytes 884740
  8.8 17.7 %copy-start.9 = (bf16[15,48,48]{2,1,0:T(8,128)(2,1)S(1)}, bf16[15,48,48]{2,1,0:T(8,128)(2,1)}, u32[]{:S(2)}) copy-start(bf16[15,48,48]{2,1,0:T(8,128)(2,1)} %param.6) | copy-start | bytes 207364
  10.5 25.7 %all-to-all-start = ((bf16[32,2,2304]{2,1,0:T(2,128)(2,1)}), bf16[32,2,2304]{2,1,0:T(2,128)(2,1)S(1)}, u32[]{:S(2)}, u32[]{:S(2)}) async-start(bf16[32,2,2304]{2,1,0:T(2,128)(2,1)} %reshape.644), calls=%async_computation | async-start | bytes 589824 | tf_op jit(solution)/shard_map/all_to_all | solution.py:66
  21.8 4.9 %copy-start.8 = (bf16[15,48,48]{2,1,0:T(8,128)(2,1)S(1)}, bf16[15,48,48]{2,1,0:T(8,128)(2,1)}, u32[]{:S(2)}) copy-start(bf16[15,48,48]{2,1,0:T(8,128)(2,1)} %param.5) | copy-start | bytes 207364
  21.9 5.5 %copy-start.2 = (bf16[3,1,48,8,128]{4,3,2,1,0:T(8,128)(2,1)S(1)}, bf16[3,1,48,8,128]{4,3,2,1,0:T(8,128)(2,1)}, u32[]{:S(2)}) copy-start(bf16[3,1,48,8,128]{4,3,2,1,0:T(8,128)(2,1)} %param.4) | copy-start | bytes 884740
  22.1 12.6 %collective-permute-start.3 = (bf16[3,1,48,8,7]{4,2,3,0,1:T(8,128)(2,1)S(1)}, bf16[3,1,48,8,7]{4,2,3,0,1:T(8,128)(2,1)S(1)}, u32[]{:S(2)}, u32[]{:S(2)}) collective-permute-start(bf16[3,1,48,8,7]{4,2,3,0,1:T(8,128)(2,1)S(1)} %get-tuple-element.24), channel_id=1, source_target_pairs={{1,0},{2,1},{3,2},{4,3},{5,4},{6,5},{7,6},{9,8},{10,9},{11,10},{12... | collective-permute-start | bytes 48392 | tf_op jit(solution)/shard_map/ppermute | solution.py:22
  24.0 8.0 %collective-permute-start.2 = (bf16[3,1,48,8,7]{4,2,3,0,1:T(8,128)(2,1)S(1)}, bf16[3,1,48,8,7]{4,2,3,0,1:T(8,128)(2,1)S(1)}, u32[]{:S(2)}, u32[]{:S(2)}) collective-permute-start(bf16[3,1,48,8,7]{4,2,3,0,1:T(8,128)(2,1)S(1)} %get-tuple-element.25), channel_id=1, source_target_pairs={{0,1},{1,2},{2,3},{3,4},{4,5},{5,6},{6,7},{8,9},{9,10},{10,11},{11... | collective-permute-start | bytes 48392 | tf_op jit(solution)/shard_map/ppermute | solution.py:20
  26.5 8.6 %copy-start.12 = (bf16[15,48,48]{1,2,0:T(8,128)(2,1)}, bf16[15,48,48]{1,2,0:T(8,128)(2,1)S(1)}, u32[]{:S(2)}) copy-start(bf16[15,48,48]{1,2,0:T(8,128)(2,1)S(1)} %reverse_bitcast_fusion.1) | copy-start | bytes 207364
  42.4 12.5 %copy-start.5 = (f32[48,3,8,128]{3,0,2,1:T(8,128)S(1)}, f32[48,3,8,128]{3,0,2,1:T(8,128)}, u32[]{:S(2)}) copy-start(f32[48,3,8,128]{3,0,2,1:T(8,128)} %fusion.6) | copy-start | bytes 1769476
  44.9 22.2 %all-to-all-start.1 = ((bf16[32,2,2304]{2,1,0:T(2,128)(2,1)}), bf16[32,2,2304]{2,1,0:T(2,128)(2,1)S(1)}, u32[]{:S(2)}, u32[]{:S(2)}) async-start(bf16[32,2,2304]{2,1,0:T(2,128)(2,1)} %reshape.646), calls=%async_computation.1 | async-start | bytes 589824 | tf_op jit(solution)/shard_map/all_to_all | solution.py:71
  67.1 16.3 %all-to-all-start.2 = ((bf16[32,2,2304]{2,1,0:T(2,128)(2,1)}), bf16[32,2,2304]{2,1,0:T(2,128)(2,1)S(1)}, u32[]{:S(2)}, u32[]{:S(2)}) async-start(bf16[32,2,2304]{2,1,0:T(2,128)(2,1)} %reshape.648), calls=%async_computation.2 | async-start | bytes 589824 | tf_op jit(solution)/shard_map/all_to_all | solution.py:72
  71.8 107.3 %all-reduce.8.cloned.1.call-start = ((), (), s32[]{:S(2)}) async-start(), calls=%async_computation.4 | async-start | bytes 1474560 | tf_op jit(solution)/shard_map/psum | solution.py:8
  74.8 6.2 %copy-start.10 = (bf16[15,48,48]{2,1,0:T(8,128)(2,1)S(1)}, bf16[15,48,48]{2,1,0:T(8,128)(2,1)}, u32[]{:S(2)}) copy-start(bf16[15,48,48]{2,1,0:T(8,128)(2,1)} %param.6) | copy-start | bytes 207364
  75.8 8.4 %copy-start.6 = (bf16[3,48,8,128]{3,1,2,0:T(8,128)(2,1)}, bf16[3,48,8,128]{3,1,2,0:T(8,128)(2,1)S(1)}, u32[]{:S(2)}) copy-start(bf16[3,48,8,128]{3,1,2,0:T(8,128)(2,1)S(1)} %copy.179) | copy-start | bytes 884740
  76.7 19.7 %collective-permute-start.1 = (bf16[3,1,48,8,7]{4,2,3,0,1:T(8,128)(2,1)}, bf16[3,1,48,8,7]{4,2,3,0,1:T(8,128)(2,1)S(1)}, u32[]{:S(2)}, u32[]{:S(2)}) collective-permute-start(bf16[3,1,48,8,7]{4,2,3,0,1:T(8,128)(2,1)} %get-tuple-element.28), channel_id=1, source_target_pairs={{1,0},{2,1},{3,2},{4,3},{5,4},{6,5},{7,6},{9,8},{10,9},{11,10},{12... | collective-permute-start | bytes 48392 | tf_op jit(solution)/shard_map/ppermute | solution.py:22
  78.6 14.6 %collective-permute-start = (bf16[3,1,48,8,7]{4,2,3,0,1:T(8,128)(2,1)}, bf16[3,1,48,8,7]{4,2,3,0,1:T(8,128)(2,1)S(1)}, u32[]{:S(2)}, u32[]{:S(2)}) collective-permute-start(bf16[3,1,48,8,7]{4,2,3,0,1:T(8,128)(2,1)} %get-tuple-element.29), channel_id=1, source_target_pairs={{0,1},{1,2},{2,3},{3,4},{4,5},{5,6},{6,7},{8,9},{9,10},{10,11},{11... | collective-permute-start | bytes 48392 | tf_op jit(solution)/shard_map/ppermute | solution.py:20
  85.9 1.9 copy-start.1
  87.9 17.3 %collective-permute-start.4 = (bf16[2,3,1,48,7,128]{5,3,4,1,2,0:T(8,128)(2,1)S(1)}, bf16[2,3,1,48,7,128]{5,3,4,1,2,0:T(8,128)(2,1)S(1)}, u32[]{:S(2)}, u32[]{:S(2)}) collective-permute-start(bf16[2,3,1,48,7,128]{5,3,4,1,2,0:T(8,128)(2,1)S(1)} %get-tuple-element.22), channel_id=1, source_target_pairs={{0,8},{8,16},{16,24},{24,32},{32,40},{40,48},{48,56},{56,64},{64,7... | collective-permute-start | bytes 1548296 | tf_op jit(solution)/shard_map/ppermute | solution.py:20
  91.7 14.8 %collective-permute-start.5 = (bf16[2,3,1,48,7,128]{5,3,4,1,2,0:T(8,128)(2,1)S(1)}, bf16[2,3,1,48,7,128]{5,3,4,1,2,0:T(8,128)(2,1)S(1)}, u32[]{:S(2)}, u32[]{:S(2)}) collective-permute-start(bf16[2,3,1,48,7,128]{5,3,4,1,2,0:T(8,128)(2,1)S(1)} %get-tuple-element.23), channel_id=1, source_target_pairs={{8,0},{16,8},{24,16},{32,24},{40,32},{48,40},{56,48},{64,56},{72,6... | collective-permute-start | bytes 1548296 | tf_op jit(solution)/shard_map/ppermute | solution.py:22
  94.6 1.1 copy-start.7
  98.9 1.1 copy-start.4
  102.0 1.0 copy-start.3
  105.2 0.7 copy-start.13
  109.3 1.2 copy-start.11
  110.5 0.7 copy-start.14
  113.2 219.5 %all-reduce.6.cloned.1.call-start = ((), (), s32[]{:S(2)}) async-start(), calls=%async_computation.3 | async-start | bytes 1474560 | tf_op jit(solution)/shard_map/psum | solution.py:9
Sparse Core Ops, SparseCore 0:
  113.3 65.7 all-reduce.7
  182.9 149.7 all-reduce.5
